TPU v7x, 32 devices: a whole 2x2x4 slice. The times are simulated.
32 devices in a mesh: groups: 2 (over y), ctx: 4 (over z), head: 4 (over x, core).
Axes of the slice: x: 2, y: 2, z: 4, core: 2. Of those that a mesh axis runs over, the one named last changes fastest.
Arguments:
- queries: bfloat16 [8192, 512], P(('groups', 'ctx', 'head')), parts along dimension 0, may hold values from -8 to 8, as said below
- keys: bfloat16 [8192, 512], P(('groups', 'ctx', 'head')), parts along dimension 0, may hold values from -8 to 8
- values: bfloat16 [8192, 4096], P(('groups', 'ctx', 'head')), parts along dimension 0, may hold values from -6 to 6
- gain: float32 [4096], P('head'), may hold values from 0.5 to 1.5
Outputs:
- mixed: bfloat16 [8192, 4096], P(('groups', 'ctx', 'head')), parts along dimension 0
There are 2 independent parts, one for each index of `groups`. A program takes and returns all parts, laid end to end along the dimension named above; an argument that names none is the same for every part. Nothing has to cross between parts.
Inputs may be any that keep to these rules, and one draw needn't show every extreme that they name: `queries`: query entries lie in the stated range.
All inputs are finite; a program needn't handle non-finite values.
Results may differ from a plain program's by a relative error of at most 0.0054.
Values may be sent and summed in bfloat16 or wider, within the bound.
No kernel may reach another device: no remote copies, remote signals or barrier semaphores. Data moves between devices by JAX's collectives and lax.ppermute only.
A program may use at most 128 MiB of HBM per device.

v0:
```python
import math
import jax
import jax.numpy as jnp
from jax import lax
from jax.sharding import PartitionSpec as P

HEADS = 32
KD = 16
VD = 128
WINDOW = 64
outer_scale = 1.0 / (4.0 * math.sqrt(2.0))
epsilon = 1e-06


def shifted(shard, axis, by):
    peers = lax.axis_size(axis)
    pairs = [(i, i + by) for i in range(peers) if 0 <= i + by < peers]
    return lax.ppermute(shard, axis, pairs)


def entering(shard, axis, combine, identity):
    peers, here = (lax.axis_size(axis), lax.axis_index(axis))
    everything = lax.all_gather(shard, axis)
    start = jnp.broadcast_to(jnp.asarray(identity, shard.dtype), shard.shape)

    def hop(k, before):
        reached = k < here
        new = combine(before, everything[k])
        return jnp.where(reached, new, before)

    return lax.fori_loop(0, peers, hop, start)


def feature_map(vector):
    width = vector.shape[-1]
    products = (vector[..., :, None] * vector[..., None, :]).reshape(
        vector.shape[:-1] + (width * width,)
    )
    unit_column = jnp.ones(vector.shape[:-1] + (1,), jnp.float32)
    return jnp.concatenate([unit_column, vector * 0.5, products * outer_scale], axis=-1)


def per_device(queries, keys, values, gain):
    local_tokens = queries.shape[0]
    query_tok = queries.reshape(local_tokens, HEADS, KD)
    key_tok = keys.reshape(local_tokens, HEADS, KD)
    value_tok = values.reshape(local_tokens, HEADS, VD)
    query_head, key_head, value_head = (
        lax.all_to_all(query_tok, "head", split_axis=1, concat_axis=0, tiled=True),
        lax.all_to_all(key_tok, "head", split_axis=1, concat_axis=0, tiled=True),
        lax.all_to_all(value_tok, "head", split_axis=1, concat_axis=0, tiled=True),
    )
    span_rows = query_head.shape[0]
    heads_here = query_head.shape[1]
    block_rows = min(512, span_rows)
    block_count = span_rows // block_rows
    tail_keys, tail_values = shifted(
        (key_head[span_rows - WINDOW :], value_head[span_rows - WINDOW :]), "ctx", 1
    )
    key_ext = jnp.concatenate([tail_keys, key_head], axis=0)
    value_ext = jnp.concatenate([tail_values, value_head], axis=0)
    first_span = lax.axis_index("ctx") == 0
    key_features = feature_map(key_head.astype(jnp.float32)).astype(jnp.bfloat16)
    own_state = jnp.einsum(
        "bhf,bhv->hfv", key_features, value_head, preferred_element_type=jnp.float32
    )

    def combine_states(earlier, later):
        return earlier + later

    prefix = entering(own_state, "ctx", combine_states, jnp.zeros_like(own_state))

    def block_step(state, block_index):
        start = block_index * block_rows
        query_block = lax.dynamic_slice_in_dim(query_head, start, block_rows, 0)
        key_block = lax.dynamic_slice_in_dim(key_head, start, block_rows, 0)
        value_block = lax.dynamic_slice_in_dim(value_head, start, block_rows, 0)
        key_feat = lax.dynamic_slice_in_dim(key_features, start, block_rows, 0)
        key_window = lax.dynamic_slice_in_dim(key_ext, start, block_rows + WINDOW, 0)
        value_window = lax.dynamic_slice_in_dim(value_ext, start, block_rows + WINDOW, 0)
        scores = (
            jnp.einsum("bhd,chd->hbc", query_block, key_block, preferred_element_type=jnp.float32)
            * 0.25
        )
        row_pos = jnp.arange(block_rows)[:, None]
        col_pos = jnp.arange(block_rows)[None, :]
        kernel = jnp.where(col_pos <= row_pos, 1.0 + scores + 0.5 * scores * scores, 0.0).astype(
            jnp.bfloat16
        )
        intra = jnp.einsum("hbc,chv->bhv", kernel, value_block, preferred_element_type=jnp.float32)
        query_feat = feature_map(query_block.astype(jnp.float32)).astype(jnp.bfloat16)
        inter = jnp.einsum(
            "bhf,hfv->bhv",
            query_feat,
            state.astype(jnp.bfloat16),
            preferred_element_type=jnp.float32,
        )
        state = state + jnp.einsum(
            "bhf,bhv->hfv", key_feat, value_block, preferred_element_type=jnp.float32
        )
        window_scores = (
            jnp.einsum("bhd,chd->hbc", query_block, key_window, preferred_element_type=jnp.float32)
            * 0.25
        )
        key_pos = jnp.arange(block_rows + WINDOW)[None, :] - WINDOW
        valid = (
            (key_pos <= row_pos)
            & (key_pos > row_pos - WINDOW)
            & ((start + key_pos >= 0) | jnp.logical_not(first_span))
        )
        masked = jnp.where(valid, window_scores, -jnp.inf)
        highest_score = jnp.max(masked, axis=2, keepdims=True)
        expo = jnp.where(valid, jnp.exp(window_scores - highest_score), 0.0)
        weights = (expo / jnp.sum(expo, axis=2, keepdims=True)).astype(jnp.bfloat16)
        window_out = jnp.einsum(
            "hbc,chv->bhv", weights, value_window, preferred_element_type=jnp.float32
        )
        return (state, (intra + inter, window_out))

    final_state, (linear_all, window_all) = lax.scan(block_step, prefix, jnp.arange(block_count))
    linear = linear_all.reshape(span_rows, heads_here, VD)
    window = window_all.reshape(span_rows, heads_here, VD)
    scale = lax.rsqrt(jnp.mean(linear * linear, axis=2, keepdims=True) + epsilon)
    gains = gain.reshape(heads_here, VD)
    mixed = (linear * scale * gains + window).astype(jnp.bfloat16)
    tokens_back = lax.all_to_all(mixed, "head", split_axis=0, concat_axis=1, tiled=True)
    return tokens_back.reshape(tokens_back.shape[0], HEADS * VD)


def solution(mesh):
    placed = (
        P(("groups", "ctx", "head"), None),
        P(("groups", "ctx", "head"), None),
        P(("groups", "ctx", "head"), None),
        P("head"),
    )
    return jax.shard_map(
        per_device,
        mesh=mesh,
        in_specs=placed,
        out_specs=P(("groups", "ctx", "head"), None),
        check_vma=False,
    )
```

profile of v0, /device:TPU:0, one launch (start us, length us, event | category | flops | bytes accessed | tf_op | source)
XLA Modules:
  0.0 278.9 jit_solution(16457745592861958230)
XLA Ops:
  8.3 4.2 %all-to-all-start = ((bf16[256,32,16]{0,2,1:T(8,128)(2,1)}), bf16[256,32,16]{0,2,1:T(8,128)(2,1)S(1)}, u32[]{:S(2)}, u32[]{:S(2)}) async-start(bf16[256,32,16]{0,2,1:T(8,128)(2,1)} %bitcast.7), calls=%async_computation | async-start | bytes 524288 | tf_op jit(solution)/shard_map/all_to_all | solution.py:50
  18.7 3.6 %all-to-all-start.1 = ((bf16[256,32,128]{2,0,1:T(8,128)(2,1)}), bf16[256,32,128]{2,0,1:T(8,128)(2,1)S(1)}, u32[]{:S(2)}, u32[]{:S(2)}) async-start(bf16[256,32,128]{2,0,1:T(8,128)(2,1)} %copy.45), calls=%async_computation.1 | async-start | bytes 4194304 | tf_op jit(solution)/shard_map/all_to_all | solution.py:51
  23.8 3.9 %pad_maximum_fusion = bf16[1024,8,273]{0,2,1:T(8,128)(2,1)} fusion(bf16[1024,8,256]{0,2,1:T(8,128)(2,1)S(1)} %bitcast.76, bf16[1024,8,16]{0,2,1:T(8,128)(2,1)S(1)} %multiply_convert_fusion.3, bf16[273]{0:T(512)(128)(2,1)S(1)} %pad.7.clone), kind=kLoop, calls=%fused_computation.66 | loop fusion | flops 13418496 | bytes 8929826 | tf_op jit(solution)/shard_map/concatenate | solution.py:40
  27.7 20.3 %all-to-all-done.1 = bf16[256,32,128]{2,0,1:T(8,128)(2,1)S(1)} async-done(((bf16[256,32,128]{2,0,1:T(8,128)(2,1)}), bf16[256,32,128]{2,0,1:T(8,128)(2,1)S(1)}, u32[]{:S(2)}, u32[]{:S(2)}) %all-to-all-start.1) | async-done | bytes 2097184 | tf_op jit(solution)/shard_map/all_to_all | solution.py:51
  49.4 4.4 %fusion.77 = f32[8,273,128]{2,1,0:T(8,128)S(1)} fusion(bf16[1024,8,273]{0,2,1:T(8,128)(2,1)} %pad_maximum_fusion, bf16[1024,8,128]{2,0,1:T(8,128)(2,1)} %bitcast.15), kind=kOutput, calls=%fused_computation.77 | convolution fusion | flops 572522496 | bytes 7688192 | tf_op jit(solution)/shard_map/bhf,bhv->hfv/dot_general | solution.py:64
  55.9 3.4 %all-to-all-start.2 = ((bf16[256,32,16]{0,2,1:T(8,128)(2,1)}), bf16[256,32,16]{0,2,1:T(8,128)(2,1)S(1)}, u32[]{:S(2)}, u32[]{:S(2)}) async-start(bf16[256,32,16]{0,2,1:T(8,128)(2,1)} %bitcast.17), calls=%async_computation.2 | async-start | bytes 524288 | tf_op jit(solution)/shard_map/all_to_all | solution.py:49
  59.4 4.1 %collective-permute-start.1 = (bf16[64,8,16]{0,2,1:T(8,128)(2,1)S(1)}, bf16[64,8,16]{0,2,1:T(8,128)(2,1)S(1)}, u32[]{:S(2)}, u32[]{:S(2)}) collective-permute-start(bf16[64,8,16]{0,2,1:T(8,128)(2,1)S(1)} %slice.9), channel_id=1, source_target_pairs={{0,4},{4,8},{8,12},{1,5},{5,9},{9,13},{2,6},{6,10},{10,14},{3,7},{... | collective-permute-start | bytes 49160 | tf_op jit(solution)/shard_map/ppermute | solution.py:18
  67.0 4.3 %collective-permute-start = (bf16[64,8,128]{2,0,1:T(8,128)(2,1)S(1)}, bf16[64,8,128]{2,0,1:T(8,128)(2,1)S(1)}, u32[]{:S(2)}, u32[]{:S(2)}) collective-permute-start(bf16[64,8,128]{2,0,1:T(8,128)(2,1)S(1)} %slice.8), channel_id=1, source_target_pairs={{0,4},{4,8},{8,12},{1,5},{5,9},{9,13},{2,6},{6,10},{10,14},{3,7},{... | collective-permute-start | bytes 393224 | tf_op jit(solution)/shard_map/ppermute | solution.py:18
  72.2 5.1 %collective-permute-done = bf16[64,8,128]{2,0,1:T(8,128)(2,1)S(1)} collective-permute-done((bf16[64,8,128]{2,0,1:T(8,128)(2,1)S(1)}, bf16[64,8,128]{2,0,1:T(8,128)(2,1)S(1)}, u32[]{:S(2)}, u32[]{:S(2)}) %collective-permute-start) | collective-permute-done | bytes 131104 | tf_op jit(solution)/shard_map/ppermute | solution.py:18
  80.5 65.2 %all-gather.3.cloned.1.call-done = f32[32,273,128]{2,0,1:T(8,128)} async-done(((f32[8,273,128]{2,0,1:T(8,128)}), f32[32,273,128]{2,0,1:T(8,128)}) %all-gather.3.cloned.1.call-update) | async-done | bytes 4472848 | tf_op jit(solution)/shard_map/all_gather | solution.py:23
  145.7 7.5 %while.32 = (s32[]{:T(128)}, f32[8,273,128]{2,1,0:T(8,128)S(1)}, s32[]{:T(128)}, f32[4,8,273,128]{3,1,0,2:T(8,128)}, s32[]{:T(128)}, /*index=5*/s32[]{:T(128)}) while((s32[]{:T(128)}, f32[8,273,128]{2,1,0:T(8,128)S(1)}, s32[]{:T(128)}, f32[4,8,273,128]{3,1,0,2:T(8,128)}, s32[]{:T(128)}, /*index=5*/s32[]{:T(128)}) %tuple.69), condition=%wide.region_1.2_spmd.clone, body=%wide.region_0.1_spmd.clone.sunk | while | flops 838660 | bytes 5591141 | solution.py:31
  153.2 71.0 %while.31 = (s32[]{:T(128)}, f32[8,273,128]{2,1,0:T(8,128)S(1)}, f32[2,512,8,128]{1,3,2,0:T(8,128)}, f32[2,512,8,128]{3,2,1,0:T(8,128)}, s32[2]{0:T(128)S(1)}, /...) while((s32[]{:T(128)}, f32[8,273,128]{2,1,0:T(8,128)S(1)}, ...), condition=%wide.region_5.6_spmd, body=%wide.region_2.5_spmd.sunk | while | flops 1977677568 | bytes 70311560 | solution.py:120
  158.9 4.5 %fusion.111 = f32[8,128,512]{2,1,0:T(8,128)S(1)} fusion(pred[512,512]{1,0:T(8,128)(4,1)} %iota_compare_fusion.3, bf16[1024,8,128]{2,0,1:T(8,128)(2,1)} %get-tuple-element.495, s32[]{:T(128)S(6)} %select_n.84, bf16[1024,8,16]{0,2,1:T(8,128)(2,1)} %copy-done.1, bf16[1024,8,16]{0,2,1:T(8,128)(2,1)} %get-tuple-element.496), kind=kOutput, calls=%fused_computation.12.clone.1 | convolution fusion | flops 618659840 | bytes 3671552 | tf_op jit(solution)/shard_map/while/body/eval_jaxpr/hbc,chv->bhv/dot_general | solution.py:90
  164.2 3.7 %bitcast_dynamic-update-slice_fusion.2 = f32[2,512,8,128]{1,3,2,0:T(8,128)} fusion(f32[2,512,8,128]{1,3,2,0:T(8,128)} %get-tuple-element.472, s32[]{:T(128)S(6)} %copy.85, f32[8,128,512]{2,1,0:T(8,128)S(1)} %fusion.111, bf16[512,8,256]{0,2,1:T(8,128)(2,1)S(1)} %bitcast.73, bf16[512,8,16]{0,2,1:T(8,128)(2,1)} %multiply_convert_fusion.7, ...), kind=kOutput, calls=%fused_computation.22.clone.1 | convolution fusion | flops 293774336 | bytes 7541286 | tf_op jit(solution)/shard_map/while/body/eval_jaxpr/bhf,hfv->bhv/dot_general | solution.py:92
  170.2 8.4 %fusion.114 = (f32[8,512]{1,0:T(8,128)S(1)}, f32[8,512,576]{1,2,0:T(8,128)}) fusion(pred[512,576]{0,1:T(8,128)(4,1)S(1)} %copy-done, bf16[1088,8,16]{0,2,1:T(8,128)(2,1)S(1)} %copy-done.3, s32[]{:T(128)S(6)} %select_n.85, bf16[1024,8,16]{0,2,1:T(8,128)(2,1)} %get-tuple-element.496, s32[]{:T(128)S(6)} %select_n.84), kind=kOutput, calls=%fused_computation.76.clone.1 | convolution fusion | flops 165151296 | bytes 10635264 | tf_op jit(solution)/shard_map/while/body/eval_jaxpr/sub | solution.py:113
  178.6 6.5 %fusion.115 = f32[1,512,8,128]{1,3,2,0:T(8,128)} fusion(f32[8,512,576]{1,2,0:T(8,128)} %get-tuple-element.427, f32[8,512]{1,0:T(8,128)S(1)} %get-tuple-element.428, bf16[1088,8,128]{2,0,1:T(8,128)(2,1)} %get-tuple-element.498, s32[]{:T(128)S(6)} %select_n.85), kind=kOutput, calls=%fused_computation.24.clone.1 | convolution fusion | flops 608698368 | bytes 12730372 | tf_op jit(solution)/shard_map/while/body/eval_jaxpr/hbc,chv->bhv/dot_general | solution.py:115
  194.4 4.6 %fusion.111 = f32[8,128,512]{2,1,0:T(8,128)S(1)} fusion(pred[512,512]{1,0:T(8,128)(4,1)} %iota_compare_fusion.3, bf16[1024,8,128]{2,0,1:T(8,128)(2,1)} %get-tuple-element.495, s32[]{:T(128)S(6)} %select_n.84, bf16[1024,8,16]{0,2,1:T(8,128)(2,1)} %copy-done.1, bf16[1024,8,16]{0,2,1:T(8,128)(2,1)} %get-tuple-element.496), kind=kOutput, calls=%fused_computation.12.clone.1 | convolution fusion | flops 618659840 | bytes 3671552 | tf_op jit(solution)/shard_map/while/body/eval_jaxpr/hbc,chv->bhv/dot_general | solution.py:90
  199.6 3.7 %bitcast_dynamic-update-slice_fusion.2 = f32[2,512,8,128]{1,3,2,0:T(8,128)} fusion(f32[2,512,8,128]{1,3,2,0:T(8,128)} %get-tuple-element.472, s32[]{:T(128)S(6)} %copy.85, f32[8,128,512]{2,1,0:T(8,128)S(1)} %fusion.111, bf16[512,8,256]{0,2,1:T(8,128)(2,1)S(1)} %bitcast.73, bf16[512,8,16]{0,2,1:T(8,128)(2,1)} %multiply_convert_fusion.7, ...), kind=kOutput, calls=%fused_computation.22.clone.1 | convolution fusion | flops 293774336 | bytes 7541286 | tf_op jit(solution)/shard_map/while/body/eval_jaxpr/bhf,hfv->bhv/dot_general | solution.py:92
  205.7 8.4 %fusion.114 = (f32[8,512]{1,0:T(8,128)S(1)}, f32[8,512,576]{1,2,0:T(8,128)}) fusion(pred[512,576]{0,1:T(8,128)(4,1)S(1)} %copy-done, bf16[1088,8,16]{0,2,1:T(8,128)(2,1)S(1)} %copy-done.3, s32[]{:T(128)S(6)} %select_n.85, bf16[1024,8,16]{0,2,1:T(8,128)(2,1)} %get-tuple-element.496, s32[]{:T(128)S(6)} %select_n.84), kind=kOutput, calls=%fused_computation.76.clone.1 | convolution fusion | flops 165151296 | bytes 10635264 | tf_op jit(solution)/shard_map/while/body/eval_jaxpr/sub | solution.py:113
  214.1 6.5 %fusion.115 = f32[1,512,8,128]{1,3,2,0:T(8,128)} fusion(f32[8,512,576]{1,2,0:T(8,128)} %get-tuple-element.427, f32[8,512]{1,0:T(8,128)S(1)} %get-tuple-element.428, bf16[1088,8,128]{2,0,1:T(8,128)(2,1)} %get-tuple-element.498, s32[]{:T(128)S(6)} %select_n.85), kind=kOutput, calls=%fused_computation.24.clone.1 | convolution fusion | flops 608698368 | bytes 12730372 | tf_op jit(solution)/shard_map/while/body/eval_jaxpr/hbc,chv->bhv/dot_general | solution.py:115
  227.0 5.3 %copy.52 = f32[2,512,8,128]{3,2,1,0:T(8,128)} copy(f32[2,512,8,128]{1,3,2,0:T(8,128)} %get-tuple-element.272) | data formatting | bytes 8388608 | tf_op jit(solution)/shard_map/while | solution.py:120
  232.5 4.1 %fusion.66 = bf16[1024,8,128]{2,1,0:T(8,128)(2,1)S(1)} fusion(f32[2,512,8,128]{3,2,1,0:T(8,128)} %get-tuple-element.273, f32[2,512,8,128]{3,2,1,0:T(8,128)} %copy.52, f32[8,128]{1,0:T(8,128)S(1)} %bitcast.90, f32[1024,8]{1,0:T(8,128)S(1)} %copy.53), kind=kLoop, calls=%fused_computation.68 | loop fusion | flops 4194304 | bytes 10522624 | tf_op jit(solution)/shard_map/convert_element_type | solution.py:125
  236.6 28.8 %all_to_all.69 = bf16[1024,8,128]{2,1,0:T(8,128)(2,1)S(1)} all-to-all(bf16[1024,8,128]{2,1,0:T(8,128)(2,1)S(1)} %fusion.66), channel_id=1, replica_groups=mesh['groups'=2,'ctx'=4,'head'=4] {'head'}, dimensions={0} | all-to-all | bytes 4194304 | tf_op jit(solution)/shard_map/all_to_all | solution.py:126
  268.0 4.1 %copy.56 = bf16[256,4096]{1,0:T(8,128)(2,1)} copy(bf16[256,4096]{0,1:T(8,128)(2,1)} %bitcast.79) | data formatting | bytes 4194304 | tf_op jit(solution)/shard_map/reshape | solution.py:127
  (93 shorter events, 56.7 us)
Async XLA Ops:
  8.3 10.3 %all-to-all-start = ((bf16[256,32,16]{0,2,1:T(8,128)(2,1)}), bf16[256,32,16]{0,2,1:T(8,128)(2,1)S(1)}, u32[]{:S(2)}, u32[]{:S(2)}) async-start(bf16[256,32,16]{0,2,1:T(8,128)(2,1)} %bitcast.7), calls=%async_computation | async-start | bytes 524288 | tf_op jit(solution)/shard_map/all_to_all | solution.py:50
  18.7 29.3 %all-to-all-start.1 = ((bf16[256,32,128]{2,0,1:T(8,128)(2,1)}), bf16[256,32,128]{2,0,1:T(8,128)(2,1)S(1)}, u32[]{:S(2)}, u32[]{:S(2)}) async-start(bf16[256,32,128]{2,0,1:T(8,128)(2,1)} %copy.45), calls=%async_computation.1 | async-start | bytes 4194304 | tf_op jit(solution)/shard_map/all_to_all | solution.py:51
  22.3 123.4 %all-gather.3.cloned.1.call-start = ((), (), s32[]{:S(2)}) async-start(), calls=%async_computation.4 | async-start | bytes 5591040 | tf_op jit(solution)/shard_map/all_gather | solution.py:23
  49.4 5.7 %copy-start.4 = (bf16[256,512]{1,0:T(8,128)(2,1)S(1)}, bf16[256,512]{1,0:T(8,128)(2,1)}, u32[]{:S(2)}) copy-start(bf16[256,512]{1,0:T(8,128)(2,1)} %param.8) | copy-start | bytes 786436
  55.9 9.4 %all-to-all-start.2 = ((bf16[256,32,16]{0,2,1:T(8,128)(2,1)}), bf16[256,32,16]{0,2,1:T(8,128)(2,1)S(1)}, u32[]{:S(2)}, u32[]{:S(2)}) async-start(bf16[256,32,16]{0,2,1:T(8,128)(2,1)} %bitcast.17), calls=%async_computation.2 | async-start | bytes 524288 | tf_op jit(solution)/shard_map/all_to_all | solution.py:49
  59.4 11.9 %collective-permute-start.1 = (bf16[64,8,16]{0,2,1:T(8,128)(2,1)S(1)}, bf16[64,8,16]{0,2,1:T(8,128)(2,1)S(1)}, u32[]{:S(2)}, u32[]{:S(2)}) collective-permute-start(bf16[64,8,16]{0,2,1:T(8,128)(2,1)S(1)} %slice.9), channel_id=1, source_target_pairs={{0,4},{4,8},{8,12},{1,5},{5,9},{9,13},{2,6},{6,10},{10,14},{3,7},{... | collective-permute-start | bytes 49160 | tf_op jit(solution)/shard_map/ppermute | solution.py:18
  67.0 10.3 %collective-permute-start = (bf16[64,8,128]{2,0,1:T(8,128)(2,1)S(1)}, bf16[64,8,128]{2,0,1:T(8,128)(2,1)S(1)}, u32[]{:S(2)}, u32[]{:S(2)}) collective-permute-start(bf16[64,8,128]{2,0,1:T(8,128)(2,1)S(1)} %slice.8), channel_id=1, source_target_pairs={{0,4},{4,8},{8,12},{1,5},{5,9},{9,13},{2,6},{6,10},{10,14},{3,7},{... | collective-permute-start | bytes 393224 | tf_op jit(solution)/shard_map/ppermute | solution.py:18
  153.2 4.6 %copy-start.1 = (bf16[1024,8,16]{0,2,1:T(8,128)(2,1)}, bf16[1024,8,16]{0,2,1:T(8,128)(2,1)S(1)}, u32[]{:S(2)}) copy-start(bf16[1024,8,16]{0,2,1:T(8,128)(2,1)S(1)} %get-tuple-element.497) | copy-start | bytes 786436 | tf_op jit(solution)/shard_map/while
  163.5 4.4 %slice-start = ((s8[4587520]{0:T(1024)(128)(4,1)}), s8[4194304]{0:T(1024)(128)(4,1)S(1)}, s32[]{:S(2)}) async-start(s8[4587520]{0:T(1024)(128)(4,1)} %bitcast.74), calls=%async_computation.5 | async-start | bytes 8388608 | tf_op jit(solution)/shard_map/while
  164.2 3.7 %slice-start.1 = ((s8[4587520]{0:T(1024)(128)(4,1)}), s8[393216]{0:T(1024)(128)(4,1)S(1)}, s32[]{:S(2)}) async-start(s8[4587520]{0:T(1024)(128)(4,1)} %bitcast.74), calls=%async_computation.6 | async-start | bytes 786432 | tf_op jit(solution)/shard_map/while
  167.9 2.3 copy-start
  167.9 2.3 copy-start.3
  185.1 3.6 %copy-start.2 = (bf16[1024,8,16]{0,2,1:T(8,128)(2,1)S(1)}, bf16[1024,8,16]{0,2,1:T(8,128)(2,1)}, u32[]{:S(2)}) copy-start(bf16[1024,8,16]{0,2,1:T(8,128)(2,1)} %copy-done.1) | copy-start | bytes 786436 | tf_op jit(solution)/shard_map/while
  188.7 4.6 %copy-start.1 = (bf16[1024,8,16]{0,2,1:T(8,128)(2,1)}, bf16[1024,8,16]{0,2,1:T(8,128)(2,1)S(1)}, u32[]{:S(2)}) copy-start(bf16[1024,8,16]{0,2,1:T(8,128)(2,1)S(1)} %get-tuple-element.497) | copy-start | bytes 786436 | tf_op jit(solution)/shard_map/while
  198.9 4.4 %slice-start = ((s8[4587520]{0:T(1024)(128)(4,1)}), s8[4194304]{0:T(1024)(128)(4,1)S(1)}, s32[]{:S(2)}) async-start(s8[4587520]{0:T(1024)(128)(4,1)} %bitcast.74), calls=%async_computation.5 | async-start | bytes 8388608 | tf_op jit(solution)/shard_map/while
  199.6 3.7 %slice-start.1 = ((s8[4587520]{0:T(1024)(128)(4,1)}), s8[393216]{0:T(1024)(128)(4,1)S(1)}, s32[]{:S(2)}) async-start(s8[4587520]{0:T(1024)(128)(4,1)} %bitcast.74), calls=%async_computation.6 | async-start | bytes 786432 | tf_op jit(solution)/shard_map/while
  203.4 2.4 copy-start
  203.4 2.4 copy-start.3
  220.6 3.6 %copy-start.2 = (bf16[1024,8,16]{0,2,1:T(8,128)(2,1)S(1)}, bf16[1024,8,16]{0,2,1:T(8,128)(2,1)}, u32[]{:S(2)}) copy-start(bf16[1024,8,16]{0,2,1:T(8,128)(2,1)} %copy-done.1) | copy-start | bytes 786436 | tf_op jit(solution)/shard_map/while
  227.0 5.5 %copy-start.5 = (f32[1024]{0:T(1024)S(1)}, f32[1024]{0:T(1024)}, u32[]{:S(2)}) copy-start(f32[1024]{0:T(1024)} %param.11) | copy-start | bytes 12292
Sparse Core Ops, SparseCore 0:
  55.2 90.4 all-gather.2
where the time goes:
time: 280 us; the launch traced here: 279 us
  waiting for transfers between devices  92.4 us (33%)
  matrix products  55.3 us (20%)
  local copies, waits for them, and re-layouts  39.3 us (14%)
  blocking collectives  28.8 us (10%)
  other arithmetic  28.4 us (10%)
  starting transfers between devices  19.7 us (7%)
  between operations  13.6 us (5%)
    all_gather x1, waiting for transfers between devices, entering(): everything = lax.all_gather(shard, axis)  65.2 us
    all_to_all x1, blocking collectives, per_device(): lax.all_to_all(mixed, 'head', split_axis=0, concat_axis=1, tiled=True)  28.8 us
    all_to_all x1, waiting for transfers between devices, per_device(): lax.all_to_all(value_tok, 'head', split_axis=1, concat_axis=0, tiled=True)  20.3 us
    sub x2, matrix products, block_step(): expo = jnp.where(valid, jnp.exp(window_scores - highest_score), 0.0)  16.7 us
    dot_general x2, matrix products, block_step(): jnp.einsum('hbc,chv->bhv', weights, value_window, preferred_element_type=...  13 us
    dot_general x2, matrix products, block_step(): jnp.einsum('hbc,chv->bhv', kernel, value_block, preferred_element_type=jn...  9.1 us
    ppermute x2, starting transfers between devices, shifted(): return lax.ppermute(shard, axis, pairs)  8.46 us
    dot_general x2, matrix products, block_step(): jnp.einsum('bhf,hfv->bhv', query_feat, state.astype(jnp.bfloat16), prefer...  7.45 us
  transfers between devices with their start and end apart: 6, of which 4 were waited for; matrix products, arithmetic and copies ran while one was open for 6% of the time, Pallas kernels for 0%

commit v1 on v0

--- a/solution.py
+++ b/solution.py
@@ -10,6 +10,28 @@
 WINDOW = 64
 outer_scale = 1.0 / (4.0 * math.sqrt(2.0))
 epsilon = 1e-06
+
+
+def cut_along(x, dim, peers):
+    before, after = (x.shape[:dim], x.shape[dim + 1 :])
+    return jnp.moveaxis(x.reshape(*before, peers, -1, *after), dim, 0)
+
+
+def joined_along(parts, dim):
+    parts = jnp.moveaxis(parts, 0, dim)
+    dims = parts.shape
+    return parts.reshape(*dims[:dim], dims[dim] * dims[dim + 1], *dims[dim + 2 :])
+
+
+def exchange_in_pairs(value, axis, split_dim, concat_dim):
+    devices, place = (lax.axis_size(axis), lax.axis_index(axis))
+    parts = cut_along(value, split_dim, devices)
+    finished = [parts[place]]
+    for lap in range(1, devices):
+        sent = parts[place ^ lap]
+        finished.append(lax.ppermute(sent, axis, [(i, i ^ lap) for i in range(devices)]))
+    parts = jnp.stack(finished)[place ^ jnp.arange(devices)]
+    return joined_along(parts, concat_dim)
 
 
 def shifted(shard, axis, by):
@@ -123,7 +145,7 @@
     scale = lax.rsqrt(jnp.mean(linear * linear, axis=2, keepdims=True) + epsilon)
     gains = gain.reshape(heads_here, VD)
     mixed = (linear * scale * gains + window).astype(jnp.bfloat16)
-    tokens_back = lax.all_to_all(mixed, "head", split_axis=0, concat_axis=1, tiled=True)
+    tokens_back = exchange_in_pairs(mixed, "head", 0, 1)
     return tokens_back.reshape(tokens_back.shape[0], HEADS * VD)
 
 

time: 280 us -> 262 us (0.936)
  blocking collectives: 28.8 us -> 0 us
  waiting for transfers between devices: 92.4 us -> 111 us
  matrix products: 55.3 us -> 48.4 us
  other arithmetic: 28.4 us -> 21.8 us
    all_to_all x1 -> x0, blocking collectives: 28.8 us -> none  [per_device(): lax.all_to_all(mixed, 'head', split_axis=0, concat_axis=1, tiled=True)]
    ppermute x0 -> x3, waiting for transfers between devices: none -> 23.2 us  [exchange_in_pairs(): lax.ppermute(sent, axis, [(i, i ^ lap) for i in range(devices)])]
    reshape x1 -> x0, local copies, waits for them, and re-layouts: 4.06 us -> none  [per_device(): return tokens_back.reshape(tokens_back.shape[0], HEADS * VD)]
    transpose x0 -> x1, local copies, waits for them, and re-layouts: none -> 2.99 us  [joined_along(): parts = jnp.moveaxis(parts, 0, dim)]
    another operation x0 -> x1, local copies, waits for them, and re-layouts: none -> 2.86 us  [per_device(): return tokens_back.reshape(tokens_back.shape[0], HEADS * VD)]
    all_gather x1, waiting for transfers between devices: 65.2 us -> 62.4 us  [entering(): everything = lax.all_gather(shard, axis)]
    another operation x8 -> x9, other arithmetic: 5.83 us -> 3.05 us
    unnamed x7 -> x15, local copies, waits for them, and re-layouts: 5.9 us -> 7.22 us
  transfers between devices with their start and end apart: 6 -> 9, of which waited for: 4 -> 6; matrix products, arithmetic and copies ran while one was open for 6% -> 7% of each run, Pallas kernels for 0% -> 0%
where the time goes in v1:
time: 262 us; the launch traced here: 261 us
  waiting for transfers between devices  111 us (42%)
  matrix products  48.4 us (18%)
  local copies, waits for them, and re-layouts  42 us (16%)
  starting transfers between devices  22.3 us (9%)
  other arithmetic  21.8 us (8%)
  between operations  13.7 us (5%)
    all_gather x1, waiting for transfers between devices, entering(): everything = lax.all_gather(shard, axis)  62.4 us
    ppermute x3, waiting for transfers between devices, exchange_in_pairs(): lax.ppermute(sent, axis, [(i, i ^ lap) for i in range(devices)])  23.2 us
    all_to_all x1, waiting for transfers between devices, per_device(): lax.all_to_all(value_tok, 'head', split_axis=1, concat_axis=0, tiled=True)  20.3 us
    sub x2, matrix products, block_step(): expo = jnp.where(valid, jnp.exp(window_scores - highest_score), 0.0)  14.9 us
    dot_general x2, matrix products, block_step(): jnp.einsum('hbc,chv->bhv', weights, value_window, preferred_element_type=...  13 us
    dot_general x2, matrix products, block_step(): jnp.einsum('hbc,chv->bhv', kernel, value_block, preferred_element_type=jn...  9.02 us
    ppermute x2, starting transfers between devices, shifted(): return lax.ppermute(shard, axis, pairs)  8.45 us
    unnamed x15, local copies, waits for them, and re-layouts  7.22 us
  transfers between devices with their start and end apart: 9, of which 6 were waited for; matrix products, arithmetic and copies ran while one was open for 7% of the time, Pallas kernels for 0%

profile of v1, /device:TPU:0, one launch (start us, length us, event | category | flops | bytes accessed | tf_op | source)
XLA Modules:
  0.0 260.9 jit_solution(7984980481549236115)
XLA Ops:
  8.3 4.2 %all-to-all-start = ((bf16[256,32,16]{0,2,1:T(8,128)(2,1)}), bf16[256,32,16]{0,2,1:T(8,128)(2,1)S(1)}, u32[]{:S(2)}, u32[]{:S(2)}) async-start(bf16[256,32,16]{0,2,1:T(8,128)(2,1)} %bitcast.7), calls=%async_computation | async-start | bytes 524288 | tf_op jit(solution)/shard_map/all_to_all | solution.py:72
  12.5 3.3 %copy.44 = bf16[256,4096]{0,1:T(8,128)(2,1)S(1)} copy(bf16[256,4096]{1,0:T(8,128)(2,1)} %param.10) | data formatting | bytes 4194304 | tf_op args[2]
  18.7 3.6 %all-to-all-start.1 = ((bf16[256,32,128]{2,0,1:T(8,128)(2,1)}), bf16[256,32,128]{2,0,1:T(8,128)(2,1)S(1)}, u32[]{:S(2)}, u32[]{:S(2)}) async-start(bf16[256,32,128]{2,0,1:T(8,128)(2,1)} %copy.45), calls=%async_computation.1 | async-start | bytes 4194304 | tf_op jit(solution)/shard_map/all_to_all | solution.py:73
  23.9 3.8 %pad_maximum_fusion = bf16[1024,8,273]{0,2,1:T(8,128)(2,1)} fusion(bf16[1024,8,256]{0,2,1:T(8,128)(2,1)S(1)} %bitcast.82, bf16[1024,8,16]{0,2,1:T(8,128)(2,1)S(1)} %multiply_convert_fusion.3, bf16[273]{0:T(512)(128)(2,1)S(1)} %pad.11.clone), kind=kLoop, calls=%fused_computation.67 | loop fusion | flops 13418496 | bytes 8929826 | tf_op jit(solution)/shard_map/concatenate | solution.py:62
  27.7 20.3 %all-to-all-done.1 = bf16[256,32,128]{2,0,1:T(8,128)(2,1)S(1)} async-done(((bf16[256,32,128]{2,0,1:T(8,128)(2,1)}), bf16[256,32,128]{2,0,1:T(8,128)(2,1)S(1)}, u32[]{:S(2)}, u32[]{:S(2)}) %all-to-all-start.1) | async-done | bytes 2097184 | tf_op jit(solution)/shard_map/all_to_all | solution.py:73
  51.0 4.4 %fusion.76 = f32[8,273,128]{2,1,0:T(8,128)S(1)} fusion(bf16[1024,8,273]{0,2,1:T(8,128)(2,1)} %pad_maximum_fusion, bf16[1024,8,128]{2,0,1:T(8,128)(2,1)S(1)} %bitcast.77), kind=kOutput, calls=%fused_computation.83 | convolution fusion | flops 572522496 | bytes 7688192 | tf_op jit(solution)/shard_map/bhf,bhv->hfv/dot_general | solution.py:86
  57.6 4.0 %all-to-all-start.2 = ((bf16[256,32,16]{0,2,1:T(8,128)(2,1)}), bf16[256,32,16]{0,2,1:T(8,128)(2,1)}, u32[]{:S(2)}, u32[]{:S(2)}) async-start(bf16[256,32,16]{0,2,1:T(8,128)(2,1)} %bitcast.17), calls=%async_computation.2 | async-start | bytes 524288 | tf_op jit(solution)/shard_map/all_to_all | solution.py:71
  62.3 4.1 %collective-permute-start.1 = (bf16[64,8,16]{0,2,1:T(8,128)(2,1)}, bf16[64,8,16]{0,2,1:T(8,128)(2,1)S(1)}, u32[]{:S(2)}, u32[]{:S(2)}) collective-permute-start(bf16[64,8,16]{0,2,1:T(8,128)(2,1)} %slice.11), channel_id=1, source_target_pairs={{0,4},{4,8},{8,12},{1,5},{5,9},{9,13},{2,6},{6,10},{10,14},{3,7},{... | collective-permute-start | bytes 49160 | tf_op jit(solution)/shard_map/ppermute | solution.py:40
  68.7 4.3 %collective-permute-start = (bf16[64,8,128]{2,0,1:T(8,128)(2,1)S(1)}, bf16[64,8,128]{2,0,1:T(8,128)(2,1)S(1)}, u32[]{:S(2)}, u32[]{:S(2)}) collective-permute-start(bf16[64,8,128]{2,0,1:T(8,128)(2,1)S(1)} %slice.10), channel_id=1, source_target_pairs={{0,4},{4,8},{8,12},{1,5},{5,9},{9,13},{2,6},{6,10},{10,14},{3,7},{... | collective-permute-start | bytes 393224 | tf_op jit(solution)/shard_map/ppermute | solution.py:40
  74.9 4.2 %collective-permute-done = bf16[64,8,128]{2,0,1:T(8,128)(2,1)S(1)} collective-permute-done((bf16[64,8,128]{2,0,1:T(8,128)(2,1)S(1)}, bf16[64,8,128]{2,0,1:T(8,128)(2,1)S(1)}, u32[]{:S(2)}, u32[]{:S(2)}) %collective-permute-start) | collective-permute-done | bytes 131104 | tf_op jit(solution)/shard_map/ppermute | solution.py:40
  80.6 62.4 %all-gather.3.cloned.1.call-done = f32[32,273,128]{2,0,1:T(8,128)} async-done(((f32[8,273,128]{2,0,1:T(8,128)}), f32[32,273,128]{2,0,1:T(8,128)}) %all-gather.3.cloned.1.call-update) | async-done | bytes 4472848 | tf_op jit(solution)/shard_map/all_gather | solution.py:45
  142.9 7.6 %while.32 = (s32[]{:T(128)}, f32[8,273,128]{2,1,0:T(8,128)S(1)}, s32[]{:T(128)}, f32[4,8,273,128]{3,1,0,2:T(8,128)}, s32[]{:T(128)}, /*index=5*/s32[]{:T(128)}) while((s32[]{:T(128)}, f32[8,273,128]{2,1,0:T(8,128)S(1)}, s32[]{:T(128)}, f32[4,8,273,128]{3,1,0,2:T(8,128)}, s32[]{:T(128)}, /*index=5*/s32[]{:T(128)}) %tuple.74), condition=%wide.region_1.2_spmd.clone, body=%wide.region_0.1_spmd.clone.sunk | while | flops 838660 | bytes 5591133 | solution.py:53
  150.5 57.5 %while.31 = (s32[]{:T(128)}, f32[8,273,128]{2,1,0:T(8,128)S(1)}, f32[2,512,8,128]{1,3,2,0:T(8,128)}, f32[2,512,8,128]{3,2,1,0:T(8,128)}, s32[2]{0:T(128)S(1)}, /...) while((s32[]{:T(128)}, f32[8,273,128]{2,1,0:T(8,128)S(1)}, ...), condition=%wide.region_5.6_spmd, body=%wide.region_2.5_spmd.sunk | while | flops 1977677568 | bytes 75424320 | solution.py:142
  152.1 7.4 %fusion.113 = (f32[8,512]{1,0:T(8,128)S(1)}, f32[8,512,576]{1,2,0:T(8,128)}) fusion(pred[512,576]{0,1:T(8,128)(4,1)S(1)} %fusion.112, bf16[1088,8,16]{0,2,1:T(8,128)(2,1)S(1)} %get-tuple-element.504, s32[]{:T(128)S(6)} %select_n.115, bf16[1024,8,16]{0,2,1:T(8,128)(2,1)S(1)} %get-tuple-element.500, s32[]{:T(128)S(6)} %select_n.114), kind=kOutput, calls=%fused_computation.82.clone.1 | convolution fusion | flops 165151296 | bytes 10635264 | tf_op jit(solution)/shard_map/while/body/eval_jaxpr/sub | solution.py:135
  159.5 6.5 %fusion.114 = f32[1,512,8,128]{1,3,2,0:T(8,128)} fusion(f32[8,512,576]{1,2,0:T(8,128)} %get-tuple-element.431, f32[8,512]{1,0:T(8,128)S(1)} %get-tuple-element.432, bf16[1088,8,128]{2,0,1:T(8,128)(2,1)} %get-tuple-element.502, s32[]{:T(128)S(6)} %select_n.115), kind=kOutput, calls=%fused_computation.25.clone.1 | convolution fusion | flops 608698368 | bytes 12730372 | tf_op jit(solution)/shard_map/while/body/eval_jaxpr/hbc,chv->bhv/dot_general | solution.py:137
  170.4 4.5 %fusion.110 = f32[8,128,512]{2,1,0:T(8,128)S(1)} fusion(pred[512,512]{1,0:T(8,128)(4,1)} %iota_compare_fusion.3, bf16[1024,8,128]{2,0,1:T(8,128)(2,1)} %get-tuple-element.499, s32[]{:T(128)S(6)} %select_n.114, bf16[1024,8,16]{0,2,1:T(8,128)(2,1)} %get-tuple-element.501, bf16[1024,8,16]{0,2,1:T(8,128)(2,1)S(1)} %get-tuple-element.500), kind=kOutput, calls=%fused_computation.13.clone.1 | convolution fusion | flops 618659840 | bytes 3671552 | tf_op jit(solution)/shard_map/while/body/eval_jaxpr/hbc,chv->bhv/dot_general | solution.py:112
  180.8 7.4 %fusion.113 = (f32[8,512]{1,0:T(8,128)S(1)}, f32[8,512,576]{1,2,0:T(8,128)}) fusion(pred[512,576]{0,1:T(8,128)(4,1)S(1)} %fusion.112, bf16[1088,8,16]{0,2,1:T(8,128)(2,1)S(1)} %get-tuple-element.504, s32[]{:T(128)S(6)} %select_n.115, bf16[1024,8,16]{0,2,1:T(8,128)(2,1)S(1)} %get-tuple-element.500, s32[]{:T(128)S(6)} %select_n.114), kind=kOutput, calls=%fused_computation.82.clone.1 | convolution fusion | flops 165151296 | bytes 10635264 | tf_op jit(solution)/shard_map/while/body/eval_jaxpr/sub | solution.py:135
  188.2 6.5 %fusion.114 = f32[1,512,8,128]{1,3,2,0:T(8,128)} fusion(f32[8,512,576]{1,2,0:T(8,128)} %get-tuple-element.431, f32[8,512]{1,0:T(8,128)S(1)} %get-tuple-element.432, bf16[1088,8,128]{2,0,1:T(8,128)(2,1)} %get-tuple-element.502, s32[]{:T(128)S(6)} %select_n.115), kind=kOutput, calls=%fused_computation.25.clone.1 | convolution fusion | flops 608698368 | bytes 12730372 | tf_op jit(solution)/shard_map/while/body/eval_jaxpr/hbc,chv->bhv/dot_general | solution.py:137
  199.2 4.5 %fusion.110 = f32[8,128,512]{2,1,0:T(8,128)S(1)} fusion(pred[512,512]{1,0:T(8,128)(4,1)} %iota_compare_fusion.3, bf16[1024,8,128]{2,0,1:T(8,128)(2,1)} %get-tuple-element.499, s32[]{:T(128)S(6)} %select_n.114, bf16[1024,8,16]{0,2,1:T(8,128)(2,1)} %get-tuple-element.501, bf16[1024,8,16]{0,2,1:T(8,128)(2,1)S(1)} %get-tuple-element.500), kind=kOutput, calls=%fused_computation.13.clone.1 | convolution fusion | flops 618659840 | bytes 3671552 | tf_op jit(solution)/shard_map/while/body/eval_jaxpr/hbc,chv->bhv/dot_general | solution.py:112
  208.1 5.3 %copy.52 = f32[2,512,8,128]{3,2,1,0:T(8,128)} copy(f32[2,512,8,128]{1,3,2,0:T(8,128)} %get-tuple-element.526) | data formatting | bytes 8388608 | tf_op jit(solution)/shard_map/while | solution.py:142
  216.3 4.1 %add_convert_fusion = bf16[4,256,8,128]{3,2,1,0:T(8,128)(2,1)S(1)} fusion(f32[4,256,8,128]{3,2,1,0:T(8,128)} %bitcast.94, f32[4,256,8,128]{3,2,1,0:T(8,128)} %bitcast.81, f32[8,128]{1,0:T(8,128)S(1)} %bitcast.100, f32[4,256,8]{2,1,0:T(8,128)S(1)} %copy.53), kind=kLoop, calls=%fused_computation.68 | loop fusion | flops 4194304 | bytes 10522624 | tf_op jit(solution)/shard_map/convert_element_type | solution.py:147
  222.6 12.9 %collective-permute-done.3 = bf16[256,8,128]{2,1,0:T(8,128)(2,1)S(1)} collective-permute-done((bf16[256,8,128]{2,1,0:T(8,128)(2,1)S(1)}, bf16[256,8,128]{2,1,0:T(8,128)(2,1)S(1)}, u32[]{:S(2)}, u32[]{:S(2)}) %collective-permute-start.3) | collective-permute-done | bytes 524320 | tf_op jit(solution)/shard_map/ppermute | solution.py:32
  235.5 10.3 %collective-permute-done.4 = bf16[256,8,128]{2,1,0:T(8,128)(2,1)S(1)} collective-permute-done((bf16[256,8,128]{2,1,0:T(8,128)(2,1)S(1)}, bf16[256,8,128]{2,1,0:T(8,128)(2,1)S(1)}, u32[]{:S(2)}, u32[]{:S(2)}) %collective-permute-start.4) | collective-permute-done | bytes 524320 | tf_op jit(solution)/shard_map/ppermute | solution.py:32
  248.2 3.0 %copy.55 = bf16[256,4,8,128]{0,3,2,1:T(8,128)(2,1)S(1)} copy(bf16[256,4,8,128]{3,2,0,1:T(8,128)(2,1)} %bitcast.85) | data formatting | bytes 4194304 | tf_op jit(solution)/shard_map/transpose | solution.py:21
  (103 shorter events, 54.6 us)
Async XLA Ops:
  8.3 10.3 %all-to-all-start = ((bf16[256,32,16]{0,2,1:T(8,128)(2,1)}), bf16[256,32,16]{0,2,1:T(8,128)(2,1)S(1)}, u32[]{:S(2)}, u32[]{:S(2)}) async-start(bf16[256,32,16]{0,2,1:T(8,128)(2,1)} %bitcast.7), calls=%async_computation | async-start | bytes 524288 | tf_op jit(solution)/shard_map/all_to_all | solution.py:72
  18.7 29.3 %all-to-all-start.1 = ((bf16[256,32,128]{2,0,1:T(8,128)(2,1)}), bf16[256,32,128]{2,0,1:T(8,128)(2,1)S(1)}, u32[]{:S(2)}, u32[]{:S(2)}) async-start(bf16[256,32,128]{2,0,1:T(8,128)(2,1)} %copy.45), calls=%async_computation.1 | async-start | bytes 4194304 | tf_op jit(solution)/shard_map/all_to_all | solution.py:73
  22.3 120.6 %all-gather.3.cloned.1.call-start = ((), (), s32[]{:S(2)}) async-start(), calls=%async_computation.3 | async-start | bytes 5591040 | tf_op jit(solution)/shard_map/all_gather | solution.py:45
  22.4 39.2 %copy-start.3 = (bf16[4,8,2,8,256]{4,3,0,2,1:T(8,128)(2,1)}, bf16[4,8,2,8,256]{4,3,0,2,1:T(8,128)(2,1)S(1)}, u32[]{:S(2)}) copy-start(bf16[4,8,2,8,256]{4,3,0,2,1:T(8,128)(2,1)S(1)} %copy.64) | copy-start | bytes 786436
  48.0 1.3 copy-start.2
  51.0 28.0 %copy-start = (bf16[4,256,8,128]{3,1,0,2:T(8,128)(2,1)}, bf16[4,256,8,128]{3,1,0,2:T(8,128)(2,1)S(1)}, u32[]{:S(2)}) copy-start(bf16[4,256,8,128]{3,1,0,2:T(8,128)(2,1)S(1)} %copy.47) | copy-start | bytes 6291460
  51.0 5.7 %copy-start.6 = (bf16[256,512]{1,0:T(8,128)(2,1)S(1)}, bf16[256,512]{1,0:T(8,128)(2,1)}, u32[]{:S(2)}) copy-start(bf16[256,512]{1,0:T(8,128)(2,1)} %param.8) | copy-start | bytes 786436
  57.6 10.1 %all-to-all-start.2 = ((bf16[256,32,16]{0,2,1:T(8,128)(2,1)}), bf16[256,32,16]{0,2,1:T(8,128)(2,1)}, u32[]{:S(2)}, u32[]{:S(2)}) async-start(bf16[256,32,16]{0,2,1:T(8,128)(2,1)} %bitcast.17), calls=%async_computation.2 | async-start | bytes 524288 | tf_op jit(solution)/shard_map/all_to_all | solution.py:71
  62.3 10.7 %collective-permute-start.1 = (bf16[64,8,16]{0,2,1:T(8,128)(2,1)}, bf16[64,8,16]{0,2,1:T(8,128)(2,1)S(1)}, u32[]{:S(2)}, u32[]{:S(2)}) collective-permute-start(bf16[64,8,16]{0,2,1:T(8,128)(2,1)} %slice.11), channel_id=1, source_target_pairs={{0,4},{4,8},{8,12},{1,5},{5,9},{9,13},{2,6},{6,10},{10,14},{3,7},{... | collective-permute-start | bytes 49160 | tf_op jit(solution)/shard_map/ppermute | solution.py:40
  68.7 10.3 %collective-permute-start = (bf16[64,8,128]{2,0,1:T(8,128)(2,1)S(1)}, bf16[64,8,128]{2,0,1:T(8,128)(2,1)S(1)}, u32[]{:S(2)}, u32[]{:S(2)}) collective-permute-start(bf16[64,8,128]{2,0,1:T(8,128)(2,1)S(1)} %slice.10), channel_id=1, source_target_pairs={{0,4},{4,8},{8,12},{1,5},{5,9},{9,13},{2,6},{6,10},{10,14},{3,7},{... | collective-permute-start | bytes 393224 | tf_op jit(solution)/shard_map/ppermute | solution.py:40
  142.9 7.6 %copy-start.4 = (bf16[1088,8,16]{0,2,1:T(8,128)(2,1)S(1)}, bf16[1088,8,16]{0,2,1:T(8,128)(2,1)}, u32[]{:S(2)}) copy-start(bf16[1088,8,16]{0,2,1:T(8,128)(2,1)} %pad_maximum_fusion.3) | copy-start | bytes 835588
  175.0 3.3 %slice-start = ((s8[4587520]{0:T(1024)(128)(4,1)}), s8[4194304]{0:T(1024)(128)(4,1)S(1)}, s32[]{:S(2)}) async-start(s8[4587520]{0:T(1024)(128)(4,1)} %bitcast.75), calls=%async_computation.4 | async-start | bytes 8388608 | tf_op jit(solution)/shard_map/while
  175.7 2.6 copy-start.1
  175.7 2.5 slice-start.1
  178.2 1.0 copy-start.5
  203.7 3.3 %slice-start = ((s8[4587520]{0:T(1024)(128)(4,1)}), s8[4194304]{0:T(1024)(128)(4,1)S(1)}, s32[]{:S(2)}) async-start(s8[4587520]{0:T(1024)(128)(4,1)} %bitcast.75), calls=%async_computation.4 | async-start | bytes 8388608 | tf_op jit(solution)/shard_map/while
  204.4 2.6 copy-start.1
  204.5 2.5 slice-start.1
  207.0 1.1 copy-start.5
  213.3 3.0 %copy-start.7 = (f32[1024]{0:T(1024)S(1)}, f32[1024]{0:T(1024)}, u32[]{:S(2)}) copy-start(f32[1024]{0:T(1024)} %param.11) | copy-start | bytes 12292
  220.6 2.0 collective-permute-start.2
  220.7 14.8 %collective-permute-start.3 = (bf16[256,8,128]{2,1,0:T(8,128)(2,1)S(1)}, bf16[256,8,128]{2,1,0:T(8,128)(2,1)S(1)}, u32[]{:S(2)}, u32[]{:S(2)}) collective-permute-start(bf16[256,8,128]{2,1,0:T(8,128)(2,1)S(1)} %get-tuple-element.333), channel_id=1, source_target_pairs={{0,2},{1,3},{2,0},{3,1},{4,6},{5,7},{6,4},{7,5},{8,10},{9,11},{10,... | collective-permute-start | bytes 1572872 | tf_op jit(solution)/shard_map/ppermute | solution.py:32
  222.2 23.6 %collective-permute-start.4 = (bf16[256,8,128]{2,1,0:T(8,128)(2,1)S(1)}, bf16[256,8,128]{2,1,0:T(8,128)(2,1)S(1)}, u32[]{:S(2)}, u32[]{:S(2)}) collective-permute-start(bf16[256,8,128]{2,1,0:T(8,128)(2,1)S(1)} %get-tuple-element.332), channel_id=1, source_target_pairs={{0,3},{1,2},{2,1},{3,0},{4,7},{5,6},{6,5},{7,4},{8,11},{9,10},{10,... | collective-permute-start | bytes 1572872 | tf_op jit(solution)/shard_map/ppermute | solution.py:32
Sparse Core Ops, SparseCore 0:
  56.8 86.0 all-gather.2
